TPU v7x, 256 devices: a whole 4x4x8 slice. The times are simulated.
256 devices in a mesh: dp: 8 (over x, core), expert: 16 (over y, z_hi), tensor: 2 (over z_lo).
Axes of the slice: x: 4, y: 4, z: 8 (z_hi: 4, z_lo: 2; z = z_hi * 2 + z_lo), core: 2. Of those that a mesh axis runs over, the one named last changes fastest.
Arguments:
- tokens: bfloat16 [1024, 7168], P(('dp', 'expert'), 'tensor'), may hold values from -6 to 6
- upstream: bfloat16 [1024, 7168], P(('dp', 'expert'), 'tensor'), may hold values from -3 to 3
- probs: bfloat16 [1024, 8], P(('dp', 'expert')), may hold values from 0.049804688 to 0.59765625
- routing: int32 [1024, 8], P(('dp', 'expert')), may hold values from 0 to 15, all different within a row; in each aligned block of 8 rows (0 to 7, 8 to 15, ...) at most 5 rows name the same one
- row_rollout: int32 [1024], P(('dp', 'expert')), may hold values from 0 to 255
- group_ids: int32 [256], replicated, may hold values from 0 to 31
- rewards: int32 [256], replicated, may hold values from 0 to 1
- w_gate: bfloat16 [16, 7168, 2048], P('expert', None, ('dp', 'tensor')), may hold values from -0.0625 to 0.0625
- w_up: bfloat16 [16, 7168, 2048], P('expert', None, ('dp', 'tensor')), may hold values from -0.0625 to 0.0625
- w_down: bfloat16 [16, 2048, 7168], P('expert', ('dp', 'tensor')), may hold values from -0.125 to 0.125
Outputs:
- input_grad: bfloat16 [1024, 7168], P(('dp', 'expert'), 'tensor')
- route_grad: bfloat16 [1024, 8], P(('dp', 'expert'))
- grad_gate: bfloat16 [16, 7168, 2048], P('expert', None, ('dp', 'tensor'))
- grad_up: bfloat16 [16, 7168, 2048], P('expert', None, ('dp', 'tensor'))
- grad_down: bfloat16 [16, 2048, 7168], P('expert', ('dp', 'tensor'))
Inputs may be any that keep to these rules, and one draw needn't show every extreme that they name: `routing`: each row names 8 different experts. Within each aligned block of 8 rows (the tokens of one index pair of dp and expert) no expert is named by more than 5 rows, a bound that some block reaches.
All inputs are finite; a program needn't handle non-finite values.
Results may differ from a plain program's by a relative error of at most 0.025.
Values may be sent and summed in bfloat16 or wider, within the bound.
No kernel may reach another device: no remote copies, remote signals or barrier semaphores. Data moves between devices by JAX's collectives and lax.ppermute only.
A program may use at most 128 MiB of HBM per device.

v0:
```python
import jax
import jax.numpy as jnp
from jax import lax
from jax.sharding import PartitionSpec as P


def advantages(row_rollout, group_ids, rewards):
    same_group = (group_ids[:, None] == group_ids[None, :]).astype(jnp.float32)
    reward_values = rewards.astype(jnp.float32)
    group_total = jnp.dot(same_group, reward_values, precision=lax.Precision.HIGHEST)
    group_count = jnp.sum(same_group, axis=1)
    per_rollout = reward_values - group_total / group_count
    member = (
        row_rollout[:, None] == jnp.arange(per_rollout.shape[0], dtype=jnp.int32)[None, :]
    ).astype(jnp.float32)
    return jnp.dot(member, per_rollout, precision=lax.Precision.HIGHEST)


def selection(routing, probs, experts, capacity):
    route_hits = (
        routing[:, :, None] == jnp.arange(experts, dtype=jnp.int32)[None, None, :]
    ).astype(jnp.float32)
    occupied = jnp.sum(route_hits, axis=1)
    weight = jnp.einsum("rke,rk->re", route_hits, probs.astype(jnp.float32))
    before = jnp.cumsum(occupied, axis=0) - occupied
    slot_index = jnp.arange(capacity, dtype=jnp.float32)
    chosen = occupied.T[:, None, :] * (before.T[:, None, :] == slot_index[None, :, None]).astype(
        jnp.float32
    )
    return (route_hits, weight, chosen)


def shards(tokens, upstream, probs, routing, row_rollout, group_ids, rewards, w_gate, w_up, w_down):
    experts = lax.axis_size("expert")
    dp_size = lax.axis_size("dp")
    tensor_size = lax.axis_size("tensor")
    group_rows, features = tokens.shape
    routes_per_row = routing.shape[1]
    capacity = min(group_rows, 5 * group_rows * routes_per_row // (4 * experts))
    hidden_width = w_gate.shape[2]
    slots = experts * capacity
    advantage = advantages(row_rollout, group_ids, rewards)
    cotangent = (advantage[:, None] * upstream.astype(jnp.float32)).astype(jnp.bfloat16)
    route_hits, weight, chosen = selection(routing, probs, experts, capacity)
    chosen_half = chosen.astype(jnp.bfloat16)
    packed_rows = jnp.einsum(
        "ecr,rf->ecf", chosen_half, tokens, preferred_element_type=jnp.float32
    ).astype(jnp.bfloat16)
    packed_upstream = jnp.einsum(
        "ecr,rf->ecf", chosen_half, cotangent, preferred_element_type=jnp.float32
    ).astype(jnp.bfloat16)
    packed_prob = jnp.einsum("ecr,re->ec", chosen, weight).astype(jnp.bfloat16)
    arrived = (
        lax.all_to_all(packed_rows, "expert", split_axis=0, concat_axis=0, tiled=True),
        lax.all_to_all(packed_upstream, "expert", split_axis=0, concat_axis=0, tiled=True),
        lax.all_to_all(packed_prob, "expert", split_axis=0, concat_axis=0, tiled=True),
    )
    gathered = (
        lax.all_gather(
            arrived[0].reshape(1, slots, features), ("dp", "tensor"), axis=0, tiled=True
        ),
        lax.all_gather(
            arrived[1].reshape(1, slots, features), ("dp", "tensor"), axis=0, tiled=True
        ),
        lax.all_gather(arrived[2].reshape(1, slots), ("dp", "tensor"), axis=0, tiled=True),
    )
    rows_in = gathered[0].reshape(dp_size, tensor_size, experts, capacity, features)
    rows_back = gathered[1].reshape(dp_size, tensor_size, experts, capacity, features)
    slot_prob = gathered[2].reshape(dp_size, tensor_size, experts, capacity)[:, 0]
    layout = "dtecf"
    weights_in = jnp.concatenate([w_gate[0], w_up[0]], axis=1).reshape(
        tensor_size, features, 2 * hidden_width
    )
    weights_out = w_down[0].reshape(hidden_width, tensor_size, features)
    both = jnp.einsum(
        layout + ",tfk->deck", rows_in, weights_in, preferred_element_type=jnp.float32
    )
    gate = both[..., :hidden_width]
    up_part = both[..., hidden_width:]
    back_hidden = jnp.einsum(
        layout + ",htf->dech", rows_back, weights_out, preferred_element_type=jnp.float32
    )
    sigmoid_gate = jax.nn.sigmoid(gate)
    active = gate * sigmoid_gate
    hidden = (active * up_part).astype(jnp.bfloat16)
    hidden_wide = lax.optimization_barrier(hidden).astype(jnp.float32)
    route_part = jnp.sum(hidden_wide * back_hidden, axis=-1)
    scale = slot_prob.astype(jnp.float32)[..., None]
    scaled = scale * back_hidden
    grad_gate_in = scaled * up_part * sigmoid_gate * (1.0 + gate * (1.0 - sigmoid_gate))
    grad_up_in = scaled * active
    grad_inner = jnp.concatenate([grad_gate_in, grad_up_in], axis=-1).astype(jnp.bfloat16)
    weighted = (scale * hidden_wide).astype(jnp.bfloat16)
    grad_down = jnp.einsum(
        "dech," + layout + "->htf", weighted, rows_back, preferred_element_type=jnp.float32
    )
    grad_down = grad_down.reshape(hidden_width, tensor_size * features).astype(jnp.bfloat16)
    grad_both = jnp.einsum(
        layout + ",deck->tfk", rows_in, grad_inner, preferred_element_type=jnp.float32
    )
    grad_both = grad_both.reshape(tensor_size * features, 2 * hidden_width)
    grad_gate = grad_both[:, :hidden_width].astype(jnp.bfloat16)
    grad_up = grad_both[:, hidden_width:].astype(jnp.bfloat16)
    route_total = lax.psum(route_part, ("dp", "tensor"))
    own_route = lax.dynamic_index_in_dim(route_total, lax.axis_index("dp"), 0, keepdims=False)
    first = jnp.int32(0) // slots
    needed = min(
        dp_size,
        (slots * lax.axis_size(("dp", "tensor")) // slots + tensor_size - 1) // tensor_size + 1,
    )
    lead = jnp.clip(first // tensor_size, 0, dp_size - needed)
    part = lax.dynamic_slice_in_dim(grad_inner, lead, needed, 0)
    product = jnp.einsum("deck,tfk->dtecf", part, weights_in, preferred_element_type=jnp.float32)
    product = product.reshape(needed * tensor_size * slots, features)
    own_rows = lax.psum_scatter(
        product.astype(jnp.bfloat16), ("dp", "tensor"), scatter_dimension=0, tiled=True
    ).astype(jnp.float32)
    home = (
        lax.all_to_all(
            own_rows.reshape(experts, capacity, features).astype(jnp.bfloat16),
            "expert",
            split_axis=0,
            concat_axis=0,
            tiled=True,
        ),
        lax.all_to_all(
            own_route.astype(jnp.bfloat16), "expert", split_axis=0, concat_axis=0, tiled=True
        ),
    )
    input_grad = jnp.einsum(
        "ecr,ecf->rf", chosen_half, home[0], preferred_element_type=jnp.float32
    ).astype(jnp.bfloat16)
    per_expert = jnp.einsum("ecr,ec->re", chosen, home[1].astype(jnp.float32))
    route_grad = jnp.einsum("rke,re->rk", route_hits, per_expert).astype(jnp.bfloat16)
    return (input_grad, route_grad, grad_gate[None], grad_up[None], grad_down[None])


def solution(mesh):
    in_specs = (
        P(("dp", "expert"), "tensor"),
        P(("dp", "expert"), "tensor"),
        P(("dp", "expert"), None),
        P(("dp", "expert"), None),
        P(("dp", "expert")),
        P(),
        P(),
        P("expert", None, ("dp", "tensor")),
        P("expert", None, ("dp", "tensor")),
        P("expert", ("dp", "tensor"), None),
    )
    out_specs = (
        P(("dp", "expert"), "tensor"),
        P(("dp", "expert"), None),
        P("expert", None, ("dp", "tensor")),
        P("expert", None, ("dp", "tensor")),
        P("expert", ("dp", "tensor"), None),
    )
    return jax.shard_map(shards, mesh=mesh, in_specs=in_specs, out_specs=out_specs, check_vma=False)
```

profile of v0, /device:TPU:35, one launch (start us, length us, event | category | flops | bytes accessed | tf_op | source)
XLA Modules:
  0.0 505.4 jit_solution(11312434241959555918)
XLA Ops:
  8.9 35.1 %all_to_all.33 = bf16[16,5,3584]{2,1,0:T(8,128)(2,1)S(1)} all-to-all(bf16[16,5,3584]{2,1,0:T(8,128)(2,1)S(1)} %copy.58), channel_id=1, replica_groups=mesh['dp'=8,'expert'=16,'tensor'=2] {'expert'}, dimensions={0} | all-to-all | bytes 1146880 | tf_op jit(solution)/shard_map/all_to_all | solution.py:54
  50.9 30.4 %all_to_all.34 = bf16[16,5,3584]{2,1,0:T(8,128)(2,1)S(1)} all-to-all(bf16[16,5,3584]{2,1,0:T(8,128)(2,1)S(1)} %copy.54), channel_id=1, replica_groups=mesh['dp'=8,'expert'=16,'tensor'=2] {'expert'}, dimensions={0} | all-to-all | bytes 1146880 | tf_op jit(solution)/shard_map/all_to_all | solution.py:55
  83.3 4.2 all-to-all-start
  89.8 6.4 %all-to-all-done = bf16[16,1,5]{2,1,0:T(2,128)(2,1)S(1)} async-done(((bf16[16,1,5]{2,1,0:T(2,128)(2,1)}), bf16[16,1,5]{2,1,0:T(2,128)(2,1)S(1)}, u32[]{:S(2)}, u32[]{:S(2)}) %all-to-all-start) | async-done | bytes 192 | tf_op jit(solution)/shard_map/all_to_all | solution.py:56
  96.3 29.7 %all-gather = bf16[16,1,80]{2,1,0:T(2,128)(2,1)S(1)} all-gather(bf16[1,1,80]{2,1,0:T(2,128)(2,1)S(1)} %reshape.78), channel_id=1, replica_groups=mesh['dp'=8,'expert'=16,'tensor'=2] {'dp','tensor'}, dimensions={0}, use_global_device_ids=true | all-gather | bytes 2720 | tf_op jit(solution)/shard_map/all_gather | solution.py:65
  126.4 12.1 %copy.59 = bf16[16,80,3584]{2,0,1:T(8,128)(2,1)} copy(bf16[16,80,3584]{2,1,0:T(8,128)(2,1)} %all-gather.6.cloned.1.call-done) | data formatting | bytes 18350080 | tf_op jit(solution)/shard_map/all_gather | solution.py:59
  138.5 13.8 %reshape.76 = bf16[8,2,16,5,3584]{4,1,0,3,2:T(2,128)(2,1)} reshape(bf16[16,80,3584]{2,0,1:T(8,128)(2,1)} %copy.59) | data formatting | bytes 18350080 | tf_op jit(solution)/shard_map/reshape | solution.py:67
  152.3 35.1 %all-gather.4.cloned.1.call-done = bf16[16,80,3584]{2,1,0:T(8,128)(2,1)} async-done(((bf16[1,80,3584]{2,1,0:T(8,128)(2,1)}), bf16[16,80,3584]{2,1,0:T(8,128)(2,1)}) %all-gather.4.cloned.1.call-update) | async-done | bytes 9175056 | tf_op jit(solution)/shard_map/all_gather | solution.py:62
  187.4 12.1 %copy.55 = bf16[16,80,3584]{2,0,1:T(8,128)(2,1)} copy(bf16[16,80,3584]{2,1,0:T(8,128)(2,1)} %all-gather.4.cloned.1.call-done) | data formatting | bytes 18350080 | tf_op jit(solution)/shard_map/all_gather | solution.py:62
  199.5 13.9 %reshape.74 = bf16[8,2,16,5,3584]{4,1,0,3,2:T(2,128)(2,1)} reshape(bf16[16,80,3584]{2,0,1:T(8,128)(2,1)} %copy.55) | data formatting | bytes 18350080 | tf_op jit(solution)/shard_map/reshape | solution.py:68
  213.4 9.5 %fusion.23 = f32[8,16,5,256]{3,1,2,0:T(8,128)S(1)} fusion(bf16[2,3584,128]{2,1,0:T(8,128)(2,1)S(1)} %bitcast.121, bf16[2,3584,128]{2,1,0:T(8,128)(2,1)} %bitcast.123, bf16[8,2,16,5,3584]{4,1,0,3,2:T(2,128)(2,1)} %reshape.76), kind=kOutput, calls=%fused_computation.23 | convolution fusion | flops 2356150272 | bytes 13500416 | tf_op jit(solution)/shard_map/dtecf,tfk->deck/dot_general | solution.py:75
  222.9 5.1 %multiply_convert_fusion.2 = (bf16[8,16,5,128]{3,1,2,0:T(8,128)(2,1)S(1)}, bf16[8,16,5,128]{3,1,2,0:T(8,128)(2,1)S(1)}, bf16[8,16,5,128]{3,1,2,0:T(8,128)(2,1)S(1)}, f32[8,16,5,128]{3,1,2,0:T(8,128)S(1)}) fusion(f32[8,16,5,256]{3,1,2,0:T(8,128)S(1)} %fusion.23, f32[8,16,5]{1,2,0:T(8,128)S(1)} %copy.53, bf16[128,2,3584,1,1]{2,1,0,4,3:T(2,128)(2,1)S(1)} %bitcast.108, ...), kind=kOutput, calls=%fused_computation.39 | convolution fusion | flops 1175715840 | bytes 12487168 | tf_op jit(solution)/shard_map/dtecf,htf->dech/dot_general | solution.py:80
  228.0 3.0 convert_bitcast_fusion
  231.1 11.2 %copy.61 = bf16[8,2,16,5,3584]{4,3,2,1,0:T(8,128)(2,1)} copy(bf16[8,2,16,5,3584]{4,2,3,0,1:T(8,128)(2,1)S(1)} %convert_bitcast_fusion) | data formatting | bytes 18350080 | tf_op jit(solution)/shard_map/convert_element_type | solution.py:116
  242.3 14.9 %convert_element_type.102 = bf16[1280,3584]{1,0:T(8,128)(2,1)} reshape(bf16[8,2,16,5,3584]{4,3,2,1,0:T(8,128)(2,1)} %copy.61) | data formatting | bytes 18350080 | tf_op jit(solution)/shard_map/convert_element_type | solution.py:116
  257.2 15.2 %reshape.104 = bf16[7168,5,8,16]{0,2,1,3:T(8,128)(2,1)} reshape(bf16[2,3584,5,8,16]{1,0,3,2,4:T(2,128)(2,1)} %bitcast.107) | data formatting | bytes 18350080 | tf_op jit(solution)/shard_map/dtecf,deck->tfk/dot_general | solution.py:98
  272.7 51.8 %psum.7 = bf16[8,16,5]{1,2,0:T(8,128)(2,1)S(1)} all-reduce(f32[8,16,5]{1,2,0:T(8,128)S(1)} %get-tuple-element.11), channel_id=1, replica_groups=mesh['dp'=8,'expert'=16,'tensor'=2] {'dp','tensor'}, use_global_device_ids=true, to_apply=%region_5.6 | all-reduce | flops 640 | bytes 3840 | tf_op jit(solution)/shard_map/psum | solution.py:104
  325.2 8.6 %all-to-all-start.4 = ((bf16[16,1,5]{2,1,0:T(2,128)(2,1)}), bf16[16,1,5]{2,1,0:T(2,128)(2,1)S(1)}, u32[]{:S(2)}, u32[]{:S(2)}) async-start(bf16[16,1,5]{2,1,0:T(2,128)(2,1)} %copy.63), calls=%async_computation.5 | async-start | bytes 16384 | tf_op jit(solution)/shard_map/all_to_all | solution.py:126
  333.8 10.7 %fusion.7 = bf16[7168,256]{1,0:T(8,128)(2,1)S(1)} fusion(bf16[7168,5,8,16]{0,2,1,3:T(8,128)(2,1)} %reshape.104, bf16[8,16,5,128]{3,1,2,0:T(8,128)(2,1)S(1)} %get-tuple-element.8, bf16[8,16,5,128]{3,1,2,0:T(8,128)(2,1)S(1)} %get-tuple-element.7), kind=kOutput, calls=%fused_computation.9 | convolution fusion | flops 2351300608 | bytes 13172736 | tf_op jit(solution)/shard_map/dtecf,deck->tfk/dot_general | solution.py:98
  346.6 15.2 %reshape.105 = bf16[7168,5,8,16]{0,2,1,3:T(8,128)(2,1)} reshape(bf16[2,3584,5,8,16]{1,0,3,2,4:T(2,128)(2,1)} %bitcast.106) | data formatting | bytes 18350080 | tf_op jit(solution)/shard_map/dech,dtecf->htf/dot_general | solution.py:94
  361.8 97.4 %reduce-scatter.2.cloned.1.call-done = bf16[80,3584]{1,0:T(8,128)(2,1)} async-done(((bf16[1280,3584]{1,0:T(8,128)(2,1)}), bf16[80,3584]{1,0:T(8,128)(2,1)}) %reduce-scatter.2.cloned.1.call-update) | async-done | bytes 573456 | tf_op jit(solution)/shard_map/reduce_scatter | solution.py:115
  461.4 9.5 %all-to-all-start.3 = ((bf16[16,5,3584]{2,1,0:T(8,128)(2,1)}), bf16[16,5,3584]{2,1,0:T(8,128)(2,1)S(1)}, u32[]{:S(2)}, u32[]{:S(2)}) async-start(bf16[16,5,3584]{2,1,0:T(8,128)(2,1)} %convert_element_type.103), calls=%async_computation.4 | async-start | bytes 1835008 | tf_op jit(solution)/shard_map/all_to_all | solution.py:119
  471.0 10.6 %fusion.16 = bf16[1,128,7168]{2,1,0:T(8,128)(2,1)} fusion(bf16[7168,5,8,16]{0,2,1,3:T(8,128)(2,1)} %reshape.105, bf16[8,16,5,128]{3,1,2,0:T(8,128)(2,1)S(1)} %get-tuple-element.10), kind=kOutput, calls=%fused_computation.12 | convolution fusion | flops 1175322624 | bytes 11173888 | tf_op jit(solution)/shard_map/dech,dtecf->htf/dot_general | solution.py:94
  482.7 15.0 %all-to-all-done.3 = bf16[16,5,3584]{2,1,0:T(8,128)(2,1)S(1)} async-done(((bf16[16,5,3584]{2,1,0:T(8,128)(2,1)}), bf16[16,5,3584]{2,1,0:T(8,128)(2,1)S(1)}, u32[]{:S(2)}, u32[]{:S(2)}) %all-to-all-start.3) | async-done | bytes 573472 | tf_op jit(solution)/shard_map/all_to_all | solution.py:119
  (63 shorter events, 20.5 us)
Async XLA Ops:
  7.2 1.0 copy-start
  7.2 75.2 %copy-start.5 = (s32[8,8]{1,0:T(8,128)S(1)}, s32[8,8]{1,0:T(8,128)}, u32[]{:S(2)}) copy-start(s32[8,8]{1,0:T(8,128)} %param.13) | copy-start | bytes 772
  7.2 75.2 %copy-start.8 = (bf16[8,8]{1,0:T(8,128)(2,1)S(1)}, bf16[8,8]{1,0:T(8,128)(2,1)}, u32[]{:S(2)}) copy-start(bf16[8,8]{1,0:T(8,128)(2,1)} %param.12) | copy-start | bytes 388
  7.2 80.3 %copy-start.3 = (bf16[1,128,7168]{2,1,0:T(8,128)(2,1)S(1)}, bf16[1,128,7168]{2,1,0:T(8,128)(2,1)}, u32[]{:S(2)}) copy-start(bf16[1,128,7168]{2,1,0:T(8,128)(2,1)} %param.19) | copy-start | bytes 5505028
  7.2 119.2 %all-gather.6.cloned.1.call-start = ((), (), s32[]{:S(2)}) async-start(), calls=%async_computation.7 | async-start | bytes 9748480 | tf_op jit(solution)/shard_map/all_gather | solution.py:59
  45.1 142.3 %all-gather.4.cloned.1.call-start = ((), (), s32[]{:S(2)}) async-start(), calls=%async_computation.6 | async-start | bytes 9748480 | tf_op jit(solution)/shard_map/all_gather | solution.py:62
  83.3 12.9 %all-to-all-start = ((bf16[16,1,5]{2,1,0:T(2,128)(2,1)}), bf16[16,1,5]{2,1,0:T(2,128)(2,1)S(1)}, u32[]{:S(2)}, u32[]{:S(2)}) async-start(bf16[16,1,5]{2,1,0:T(2,128)(2,1)} %copy.52), calls=%async_computation | async-start | bytes 16384 | tf_op jit(solution)/shard_map/all_to_all | solution.py:56
  87.5 371.7 %reduce-scatter.2.cloned.1.call-start = ((), (), s32[]{:S(2)}) async-start(), calls=%async_computation.8 | async-start | bytes 9748480 | tf_op jit(solution)/shard_map/reduce_scatter | solution.py:115
  199.5 13.9 %copy-start.6 = (bf16[1,7168,128]{2,1,0:T(8,128)(2,1)S(1)}, bf16[1,7168,128]{2,1,0:T(8,128)(2,1)}, u32[]{:S(2)}) copy-start(bf16[1,7168,128]{2,1,0:T(8,128)(2,1)} %param.18) | copy-start | bytes 5505028
  213.4 9.6 %copy-start.2 = (bf16[8,2,16,5,3584]{4,1,0,3,2:T(2,128)(2,1)S(1)}, bf16[8,2,16,5,3584]{4,1,0,3,2:T(2,128)(2,1)}, u32[]{:S(2)}) copy-start(bf16[8,2,16,5,3584]{4,1,0,3,2:T(2,128)(2,1)} %reshape.74) | copy-start | bytes 27525124
  213.4 9.6 %copy-start.4 = (bf16[128,2,3584]{2,1,0:T(2,128)(2,1)S(1)}, bf16[128,2,3584]{2,1,0:T(2,128)(2,1)}, u32[]{:S(2)}) copy-start(bf16[128,2,3584]{2,1,0:T(2,128)(2,1)} %reshape_squeeze.3) | copy-start | bytes 5505028
  222.9 5.1 %copy-start.7 = (bf16[1,7168,128]{2,1,0:T(8,128)(2,1)S(1)}, bf16[1,7168,128]{2,1,0:T(8,128)(2,1)}, u32[]{:S(2)}) copy-start(bf16[1,7168,128]{2,1,0:T(8,128)(2,1)} %param.17) | copy-start | bytes 5505028
  325.2 136.2 %all-to-all-start.4 = ((bf16[16,1,5]{2,1,0:T(2,128)(2,1)}), bf16[16,1,5]{2,1,0:T(2,128)(2,1)S(1)}, u32[]{:S(2)}, u32[]{:S(2)}) async-start(bf16[16,1,5]{2,1,0:T(2,128)(2,1)} %copy.63), calls=%async_computation.5 | async-start | bytes 16384 | tf_op jit(solution)/shard_map/all_to_all | solution.py:126
  346.6 152.1 %copy-start.1 = (bf16[8,3584]{1,0:T(8,128)(2,1)S(1)}, bf16[8,3584]{1,0:T(8,128)(2,1)}, u32[]{:S(2)}) copy-start(bf16[8,3584]{1,0:T(8,128)(2,1)} %param.10) | copy-start | bytes 172036
  461.4 36.3 %all-to-all-start.3 = ((bf16[16,5,3584]{2,1,0:T(8,128)(2,1)}), bf16[16,5,3584]{2,1,0:T(8,128)(2,1)S(1)}, u32[]{:S(2)}, u32[]{:S(2)}) async-start(bf16[16,5,3584]{2,1,0:T(8,128)(2,1)} %convert_element_type.103), calls=%async_computation.4 | async-start | bytes 1835008 | tf_op jit(solution)/shard_map/all_to_all | solution.py:119
Sparse Core Ops, SparseCore 0:
  45.2 76.4 all-gather.5
  124.1 63.2 all-gather.3
  257.3 201.8 reduce-scatter.1
where the time goes:
time: 511 us; the launch traced here: 505 us
  waiting for transfers between devices  154 us (30%)
  blocking collectives  147 us (29%)
  local copies, waits for them, and re-layouts  120 us (23%)
  matrix products  43.7 us (9%)
  starting transfers between devices  22.4 us (4%)
  between operations  14.3 us (3%)
    reduce_scatter x1, waiting for transfers between devices, shards(): lax.psum_scatter(product.astype(jnp.bfloat16), ('dp', 'tensor'), scatter_...  97.4 us
    psum x1, blocking collectives, shards(): route_total = lax.psum(route_part, ('dp', 'tensor'))  51.8 us
    all_to_all x1, blocking collectives, shards(): lax.all_to_all(packed_rows, 'expert', split_axis=0, concat_axis=0, tiled=...  35.1 us
    all_gather x1, waiting for transfers between devices, shards(): lax.all_gather(arrived[1].reshape(1, slots, features), ('dp', 'tensor'),...  35.1 us
    all_to_all x1, blocking collectives, shards(): lax.all_to_all(packed_upstream, 'expert', split_axis=0, concat_axis=0, ti...  30.4 us
    all_gather x1, blocking collectives, shards(): lax.all_gather(arrived[2].reshape(1, slots), ('dp', 'tensor'), axis=0, ti...  29.7 us
    convert_element_type x2, local copies, waits for them, and re-layouts, shards(): product.astype(jnp.bfloat16)  26.1 us
    dot_general x1, local copies, waits for them, and re-layouts, shards(): jnp.einsum('dech,' + layout + '->htf', weighted, rows_back, preferred_ele...  15.2 us
  transfers between devices with their start and end apart: 6, of which 4 were waited for; matrix products, arithmetic and copies ran while one was open for 19% of the time, Pallas kernels for 0%

commit v1 on v0

--- a/solution.py
+++ b/solution.py
@@ -101,7 +101,8 @@
     grad_both = grad_both.reshape(tensor_size * features, 2 * hidden_width)
     grad_gate = grad_both[:, :hidden_width].astype(jnp.bfloat16)
     grad_up = grad_both[:, hidden_width:].astype(jnp.bfloat16)
-    route_total = lax.psum(route_part, ("dp", "tensor"))
+    blocks = lax.all_gather(route_part, ("dp", "tensor"))
+    route_total = jnp.sum(blocks, axis=0)
     own_route = lax.dynamic_index_in_dim(route_total, lax.axis_index("dp"), 0, keepdims=False)
     first = jnp.int32(0) // slots
     needed = min(

time: 511 us -> 513 us (level)
  waiting for transfers between devices: 154 us -> 178 us
  blocking collectives: 147 us -> 124 us
    psum x1 -> x0, blocking collectives: 51.8 us -> none  [shards(): route_total = lax.psum(route_part, ('dp', 'tensor'))]
    all_gather x0 -> x1, blocking collectives: none -> 28.4 us  [shards(): blocks = lax.all_gather(route_part, ('dp', 'tensor'))]
    reduce_scatter x1, waiting for transfers between devices: 97.4 us -> 121 us  [shards(): lax.psum_scatter(product.astype(jnp.bfloat16), ('dp', 'tensor'), scatter_...]
where the time goes in v1:
time: 513 us; the launch traced here: 506 us
  waiting for transfers between devices  178 us (35%)
  blocking collectives  124 us (24%)
  local copies, waits for them, and re-layouts  120 us (23%)
  matrix products  43.7 us (9%)
  starting transfers between devices  22.5 us (4%)
  between operations  14.3 us (3%)
    reduce_scatter x1, waiting for transfers between devices, shards(): lax.psum_scatter(product.astype(jnp.bfloat16), ('dp', 'tensor'), scatter_...  121 us
    all_to_all x1, blocking collectives, shards(): lax.all_to_all(packed_rows, 'expert', split_axis=0, concat_axis=0, tiled=...  35.1 us
    all_gather x1, waiting for transfers between devices, shards(): lax.all_gather(arrived[1].reshape(1, slots, features), ('dp', 'tensor'),...  35.1 us
    all_to_all x1, blocking collectives, shards(): lax.all_to_all(packed_upstream, 'expert', split_axis=0, concat_axis=0, ti...  30.4 us
    all_gather x1, blocking collectives, shards(): lax.all_gather(arrived[2].reshape(1, slots), ('dp', 'tensor'), axis=0, ti...  29.7 us
    all_gather x1, blocking collectives, shards(): blocks = lax.all_gather(route_part, ('dp', 'tensor'))  28.4 us
    convert_element_type x2, local copies, waits for them, and re-layouts, shards(): product.astype(jnp.bfloat16)  26.1 us
    dot_general x1, local copies, waits for them, and re-layouts, shards(): jnp.einsum(layout + ',deck->tfk', rows_in, grad_inner, preferred_element_...  15.2 us
  transfers between devices with their start and end apart: 6, of which 4 were waited for; matrix products, arithmetic and copies ran while one was open for 19% of the time, Pallas kernels for 0%

profile of v1, /device:TPU:35, one launch (start us, length us, event | category | flops | bytes accessed | tf_op | source)
XLA Modules:
  0.0 505.8 jit_solution(16180355695597725093)
XLA Ops:
  8.9 35.1 %all_to_all.33 = bf16[16,5,3584]{2,1,0:T(8,128)(2,1)S(1)} all-to-all(bf16[16,5,3584]{2,1,0:T(8,128)(2,1)S(1)} %copy.95), channel_id=1, replica_groups=mesh['dp'=8,'expert'=16,'tensor'=2] {'expert'}, dimensions={0} | all-to-all | bytes 1146880 | tf_op jit(solution)/shard_map/all_to_all | solution.py:54
  50.9 30.4 %all_to_all.34 = bf16[16,5,3584]{2,1,0:T(8,128)(2,1)S(1)} all-to-all(bf16[16,5,3584]{2,1,0:T(8,128)(2,1)S(1)} %copy.91), channel_id=1, replica_groups=mesh['dp'=8,'expert'=16,'tensor'=2] {'expert'}, dimensions={0} | all-to-all | bytes 1146880 | tf_op jit(solution)/shard_map/all_to_all | solution.py:55
  83.3 4.2 all-to-all-start
  89.8 6.4 %all-to-all-done = bf16[16,1,5]{2,1,0:T(2,128)(2,1)S(1)} async-done(((bf16[16,1,5]{2,1,0:T(2,128)(2,1)}), bf16[16,1,5]{2,1,0:T(2,128)(2,1)S(1)}, u32[]{:S(2)}, u32[]{:S(2)}) %all-to-all-start) | async-done | bytes 192 | tf_op jit(solution)/shard_map/all_to_all | solution.py:56
  96.3 29.7 %all-gather.1 = bf16[16,1,80]{2,1,0:T(2,128)(2,1)S(1)} all-gather(bf16[1,1,80]{2,1,0:T(2,128)(2,1)S(1)} %reshape.79), channel_id=1, replica_groups=mesh['dp'=8,'expert'=16,'tensor'=2] {'dp','tensor'}, dimensions={0}, use_global_device_ids=true | all-gather | bytes 2720 | tf_op jit(solution)/shard_map/all_gather | solution.py:65
  126.4 12.1 %copy.96 = bf16[16,80,3584]{2,0,1:T(8,128)(2,1)} copy(bf16[16,80,3584]{2,1,0:T(8,128)(2,1)} %all-gather.7.cloned.1.call-done) | data formatting | bytes 18350080 | tf_op jit(solution)/shard_map/all_gather | solution.py:59
  138.5 13.8 %reshape.76 = bf16[8,2,16,5,3584]{4,1,0,3,2:T(2,128)(2,1)} reshape(bf16[16,80,3584]{2,0,1:T(8,128)(2,1)} %copy.96) | data formatting | bytes 18350080 | tf_op jit(solution)/shard_map/reshape | solution.py:67
  152.3 35.1 %all-gather.5.cloned.1.call-done = bf16[16,80,3584]{2,1,0:T(8,128)(2,1)} async-done(((bf16[1,80,3584]{2,1,0:T(8,128)(2,1)}), bf16[16,80,3584]{2,1,0:T(8,128)(2,1)}) %all-gather.5.cloned.1.call-update) | async-done | bytes 9175056 | tf_op jit(solution)/shard_map/all_gather | solution.py:62
  187.4 12.1 %copy.92 = bf16[16,80,3584]{2,0,1:T(8,128)(2,1)} copy(bf16[16,80,3584]{2,1,0:T(8,128)(2,1)} %all-gather.5.cloned.1.call-done) | data formatting | bytes 18350080 | tf_op jit(solution)/shard_map/all_gather | solution.py:62
  199.5 13.9 %reshape.74 = bf16[8,2,16,5,3584]{4,1,0,3,2:T(2,128)(2,1)} reshape(bf16[16,80,3584]{2,0,1:T(8,128)(2,1)} %copy.92) | data formatting | bytes 18350080 | tf_op jit(solution)/shard_map/reshape | solution.py:68
  213.4 9.5 %fusion.23 = f32[8,16,5,256]{3,1,2,0:T(8,128)S(1)} fusion(bf16[2,3584,128]{2,1,0:T(8,128)(2,1)S(1)} %bitcast.125, bf16[2,3584,128]{2,1,0:T(8,128)(2,1)} %bitcast.127, bf16[8,2,16,5,3584]{4,1,0,3,2:T(2,128)(2,1)} %reshape.76), kind=kOutput, calls=%fused_computation.23 | convolution fusion | flops 2356150272 | bytes 13500416 | tf_op jit(solution)/shard_map/dtecf,tfk->deck/dot_general | solution.py:75
  222.9 5.1 %multiply_convert_fusion.2 = (bf16[8,16,5,128]{3,1,2,0:T(8,128)(2,1)S(1)}, bf16[8,16,5,128]{3,1,2,0:T(8,128)(2,1)S(1)}, bf16[8,16,5,128]{3,1,2,0:T(8,128)(2,1)S(1)}, f32[8,16,5,128]{3,1,2,0:T(8,128)S(1)}) fusion(f32[8,16,5,256]{3,1,2,0:T(8,128)S(1)} %fusion.23, f32[8,16,5]{1,2,0:T(8,128)S(1)} %copy.90, bf16[128,2,3584,1,1]{2,1,0,4,3:T(2,128)(2,1)S(1)} %bitcast.111, ...), kind=kOutput, calls=%fused_computation.40 | convolution fusion | flops 1175715840 | bytes 12487168 | tf_op jit(solution)/shard_map/dtecf,htf->dech/dot_general | solution.py:80
  228.0 3.0 convert_bitcast_fusion
  231.1 11.2 %copy.98 = bf16[8,2,16,5,3584]{4,3,2,1,0:T(8,128)(2,1)} copy(bf16[8,2,16,5,3584]{4,2,3,0,1:T(8,128)(2,1)S(1)} %convert_bitcast_fusion) | data formatting | bytes 18350080 | tf_op jit(solution)/shard_map/convert_element_type | solution.py:117
  242.3 14.9 %convert_element_type.102 = bf16[1280,3584]{1,0:T(8,128)(2,1)} reshape(bf16[8,2,16,5,3584]{4,3,2,1,0:T(8,128)(2,1)} %copy.98) | data formatting | bytes 18350080 | tf_op jit(solution)/shard_map/convert_element_type | solution.py:117
  257.5 28.4 %all-gather = f32[128,16,5]{1,0,2:T(8,128)S(1)} all-gather(f32[8,16,5]{1,0,2:T(8,128)S(1)} %copy.100), channel_id=2, replica_groups=mesh['dp'=8,'expert'=16,'tensor'=2] {'dp','tensor'}, dimensions={0}, use_global_device_ids=true | all-gather | bytes 43520 | tf_op jit(solution)/shard_map/all_gather | solution.py:104
  286.7 8.9 %all-to-all-start.4 = ((bf16[16,1,5]{2,1,0:T(2,128)(2,1)}), bf16[16,1,5]{2,1,0:T(2,128)(2,1)S(1)}, u32[]{:S(2)}, u32[]{:S(2)}) async-start(bf16[16,1,5]{2,1,0:T(2,128)(2,1)} %copy.101), calls=%async_computation.5 | async-start | bytes 16384 | tf_op jit(solution)/shard_map/all_to_all | solution.py:127
  295.6 15.2 %reshape.105 = bf16[7168,5,8,16]{0,2,1,3:T(8,128)(2,1)} reshape(bf16[2,3584,5,8,16]{1,0,3,2,4:T(2,128)(2,1)} %bitcast.110) | data formatting | bytes 18350080 | tf_op jit(solution)/shard_map/dtecf,deck->tfk/dot_general | solution.py:98
  310.8 10.7 %fusion.7 = bf16[7168,256]{1,0:T(8,128)(2,1)S(1)} fusion(bf16[7168,5,8,16]{0,2,1,3:T(8,128)(2,1)} %reshape.105, bf16[8,16,5,128]{3,1,2,0:T(8,128)(2,1)S(1)} %get-tuple-element.8, bf16[8,16,5,128]{3,1,2,0:T(8,128)(2,1)S(1)} %get-tuple-element.7), kind=kOutput, calls=%fused_computation.9 | convolution fusion | flops 2351300608 | bytes 13172736 | tf_op jit(solution)/shard_map/dtecf,deck->tfk/dot_general | solution.py:98
  323.6 15.2 %reshape.106 = bf16[7168,5,8,16]{0,2,1,3:T(8,128)(2,1)} reshape(bf16[2,3584,5,8,16]{1,0,3,2,4:T(2,128)(2,1)} %bitcast.109) | data formatting | bytes 18350080 | tf_op jit(solution)/shard_map/dech,dtecf->htf/dot_general | solution.py:94
  338.8 121.2 %reduce-scatter.2.cloned.1.call-done = bf16[80,3584]{1,0:T(8,128)(2,1)} async-done(((bf16[1280,3584]{1,0:T(8,128)(2,1)}), bf16[80,3584]{1,0:T(8,128)(2,1)}) %reduce-scatter.2.cloned.1.call-update) | async-done | bytes 573456 | tf_op jit(solution)/shard_map/reduce_scatter | solution.py:116
  462.2 9.4 %all-to-all-start.3 = ((bf16[16,5,3584]{2,1,0:T(8,128)(2,1)}), bf16[16,5,3584]{2,1,0:T(8,128)(2,1)S(1)}, u32[]{:S(2)}, u32[]{:S(2)}) async-start(bf16[16,5,3584]{2,1,0:T(8,128)(2,1)} %convert_element_type.103), calls=%async_computation.4 | async-start | bytes 1835008 | tf_op jit(solution)/shard_map/all_to_all | solution.py:120
  471.6 10.6 %fusion.16 = bf16[1,128,7168]{2,1,0:T(8,128)(2,1)} fusion(bf16[7168,5,8,16]{0,2,1,3:T(8,128)(2,1)} %reshape.106, bf16[8,16,5,128]{3,1,2,0:T(8,128)(2,1)S(1)} %get-tuple-element.10), kind=kOutput, calls=%fused_computation.12 | convolution fusion | flops 1175322624 | bytes 11173888 | tf_op jit(solution)/shard_map/dech,dtecf->htf/dot_general | solution.py:94
  483.3 14.8 %all-to-all-done.3 = bf16[16,5,3584]{2,1,0:T(8,128)(2,1)S(1)} async-done(((bf16[16,5,3584]{2,1,0:T(8,128)(2,1)}), bf16[16,5,3584]{2,1,0:T(8,128)(2,1)S(1)}, u32[]{:S(2)}, u32[]{:S(2)}) %all-to-all-start.3) | async-done | bytes 573472 | tf_op jit(solution)/shard_map/all_to_all | solution.py:120
  (66 shorter events, 20.6 us)
Async XLA Ops:
  7.2 1.0 copy-start
  7.2 75.2 %copy-start.5 = (s32[8,8]{1,0:T(8,128)S(1)}, s32[8,8]{1,0:T(8,128)}, u32[]{:S(2)}) copy-start(s32[8,8]{1,0:T(8,128)} %param.13) | copy-start | bytes 772
  7.2 75.2 %copy-start.8 = (bf16[8,8]{1,0:T(8,128)(2,1)S(1)}, bf16[8,8]{1,0:T(8,128)(2,1)}, u32[]{:S(2)}) copy-start(bf16[8,8]{1,0:T(8,128)(2,1)} %param.12) | copy-start | bytes 388
  7.2 80.3 %copy-start.3 = (bf16[1,128,7168]{2,1,0:T(8,128)(2,1)S(1)}, bf16[1,128,7168]{2,1,0:T(8,128)(2,1)}, u32[]{:S(2)}) copy-start(bf16[1,128,7168]{2,1,0:T(8,128)(2,1)} %param.19) | copy-start | bytes 5505028
  7.2 119.2 %all-gather.7.cloned.1.call-start = ((), (), s32[]{:S(2)}) async-start(), calls=%async_computation.7 | async-start | bytes 9748480 | tf_op jit(solution)/shard_map/all_gather | solution.py:59
  45.1 142.3 %all-gather.5.cloned.1.call-start = ((), (), s32[]{:S(2)}) async-start(), calls=%async_computation.6 | async-start | bytes 9748480 | tf_op jit(solution)/shard_map/all_gather | solution.py:62
  83.3 12.9 %all-to-all-start = ((bf16[16,1,5]{2,1,0:T(2,128)(2,1)}), bf16[16,1,5]{2,1,0:T(2,128)(2,1)S(1)}, u32[]{:S(2)}, u32[]{:S(2)}) async-start(bf16[16,1,5]{2,1,0:T(2,128)(2,1)} %copy.89), calls=%async_computation | async-start | bytes 16384 | tf_op jit(solution)/shard_map/all_to_all | solution.py:56
  87.5 372.5 %reduce-scatter.2.cloned.1.call-start = ((), (), s32[]{:S(2)}) async-start(), calls=%async_computation.8 | async-start | bytes 9748480 | tf_op jit(solution)/shard_map/reduce_scatter | solution.py:116
  199.5 13.9 %copy-start.6 = (bf16[1,7168,128]{2,1,0:T(8,128)(2,1)S(1)}, bf16[1,7168,128]{2,1,0:T(8,128)(2,1)}, u32[]{:S(2)}) copy-start(bf16[1,7168,128]{2,1,0:T(8,128)(2,1)} %param.18) | copy-start | bytes 5505028
  213.4 9.6 %copy-start.2 = (bf16[8,2,16,5,3584]{4,1,0,3,2:T(2,128)(2,1)S(1)}, bf16[8,2,16,5,3584]{4,1,0,3,2:T(2,128)(2,1)}, u32[]{:S(2)}) copy-start(bf16[8,2,16,5,3584]{4,1,0,3,2:T(2,128)(2,1)} %reshape.74) | copy-start | bytes 27525124
  213.4 9.6 %copy-start.4 = (bf16[128,2,3584]{2,1,0:T(2,128)(2,1)S(1)}, bf16[128,2,3584]{2,1,0:T(2,128)(2,1)}, u32[]{:S(2)}) copy-start(bf16[128,2,3584]{2,1,0:T(2,128)(2,1)} %reshape_squeeze.3) | copy-start | bytes 5505028
  222.9 5.1 %copy-start.7 = (bf16[1,7168,128]{2,1,0:T(8,128)(2,1)S(1)}, bf16[1,7168,128]{2,1,0:T(8,128)(2,1)}, u32[]{:S(2)}) copy-start(bf16[1,7168,128]{2,1,0:T(8,128)(2,1)} %param.17) | copy-start | bytes 5505028
  286.7 175.4 %all-to-all-start.4 = ((bf16[16,1,5]{2,1,0:T(2,128)(2,1)}), bf16[16,1,5]{2,1,0:T(2,128)(2,1)S(1)}, u32[]{:S(2)}, u32[]{:S(2)}) async-start(bf16[16,1,5]{2,1,0:T(2,128)(2,1)} %copy.101), calls=%async_computation.5 | async-start | bytes 16384 | tf_op jit(solution)/shard_map/all_to_all | solution.py:127
  323.6 175.4 %copy-start.1 = (bf16[8,3584]{1,0:T(8,128)(2,1)S(1)}, bf16[8,3584]{1,0:T(8,128)(2,1)}, u32[]{:S(2)}) copy-start(bf16[8,3584]{1,0:T(8,128)(2,1)} %param.10) | copy-start | bytes 172036
  462.2 35.9 %all-to-all-start.3 = ((bf16[16,5,3584]{2,1,0:T(8,128)(2,1)}), bf16[16,5,3584]{2,1,0:T(8,128)(2,1)S(1)}, u32[]{:S(2)}, u32[]{:S(2)}) async-start(bf16[16,5,3584]{2,1,0:T(8,128)(2,1)} %convert_element_type.103), calls=%async_computation.4 | async-start | bytes 1835008 | tf_op jit(solution)/shard_map/all_to_all | solution.py:120
Sparse Core Ops, SparseCore 0:
  45.2 76.4 all-gather.6
  124.1 63.2 all-gather.4
  257.3 202.5 reduce-scatter.1
